TPU v7x, 128 devices: a whole 4x4x4 slice. The times are simulated.
128 devices in a mesh: resp: 8 (over x_lo, y), ctx: 16 (over z, x_hi, core).
Axes of the slice: x: 4 (x_hi: 2, x_lo: 2; x = x_hi * 2 + x_lo), y: 4, z: 4, core: 2. Of those that a mesh axis runs over, the one named last changes fastest.
Arguments:
- queries: bfloat16 [64, 512, 8192], P('resp', 'ctx'), may hold values from -32 to 32
- prompt_kv: bfloat16 [2, 1024, 1024], P(None, ('resp', 'ctx')), may hold values from -4 to 4
- response_kv: bfloat16 [2, 64, 512, 1024], P(None, 'resp', 'ctx'), may hold values from -4 to 4
- lengths: int32 [64], P('resp'), may hold values from 128 to 512, as said below
Outputs:
- attended: bfloat16 [64, 512, 8192], P('resp', 'ctx')
- row_lse: float32 [64, 512, 64], P('resp', 'ctx')
Inputs may be any that keep to these rules, and one draw needn't show every extreme that they name: `lengths`: some response of every draw has length 512.
All inputs are finite; a program needn't handle non-finite values.
Results may differ from a plain program's by a relative error of at most 0.005.
Values may be sent and summed in bfloat16 or wider, within the bound.
No kernel may reach another device: no remote copies, remote signals or barrier semaphores. Data moves between devices by JAX's collectives and lax.ppermute only.
A program may use at most 256 MiB of HBM per device.

v0:
```python
import functools
import math

import jax
import jax.numpy as jnp
from jax import lax
from jax.experimental import pallas as pl
from jax.experimental.pallas import tpu as pltpu
from jax.sharding import PartitionSpec as P

HEAD = 128
NEG = -1e30


def stack_groups(q, groups):
    return jnp.concatenate([q[:, g * HEAD:(g + 1) * HEAD] for g in range(groups)], axis=0)


def scores(qk, keys, scale):
    return lax.dot_general(qk, keys, (((1,), (1,)), ((), ())), preferred_element_type=jnp.float32) * scale


def prompt_kernel(meta_ref, q_ref, pk_ref, own_ref, acc_ref, ml_ref, *, rows, groups, kv_heads, scale):
    r = pl.program_id(0)
    c = meta_ref[meta_ref.shape[0] - 1]
    length = meta_ref[r]
    nrow = rows * groups
    kv_width = groups * HEAD

    @pl.when(length > rows * c)
    def _():
        row_i = rows * c + lax.broadcasted_iota(jnp.int32, (nrow, 1), 0) % rows
        j = rows * c + lax.broadcasted_iota(jnp.int32, (nrow, rows), 1)
        live = (j <= row_i) & (j < length)
        lane = lax.broadcasted_iota(jnp.int32, (nrow, 128), 1)

        def head(k, carry):
            col = pl.multiple_of(k * HEAD, HEAD)
            qk = stack_groups(q_ref[0, :, pl.ds(pl.multiple_of(k * kv_width, kv_width), kv_width)], groups)
            s1 = scores(qk, pk_ref[0, :, pl.ds(col, HEAD)], scale)
            s2 = jnp.where(live, scores(qk, own_ref[0, 0, :, pl.ds(col, HEAD)], scale), NEG)
            m = jnp.maximum(jnp.max(s1, axis=-1, keepdims=True), jnp.max(s2, axis=-1, keepdims=True))
            p1 = jnp.exp(s1 - m)
            p2 = jnp.where(live, jnp.exp(s2 - m), 0.0)
            l = jnp.sum(p1, axis=-1, keepdims=True) + jnp.sum(p2, axis=-1, keepdims=True)
            acc = jnp.dot(p1.astype(jnp.bfloat16), pk_ref[1, :, pl.ds(col, HEAD)], preferred_element_type=jnp.float32)
            acc = acc + jnp.dot(p2.astype(jnp.bfloat16), own_ref[1, 0, :, pl.ds(col, HEAD)], preferred_element_type=jnp.float32)
            acc_ref[0, k] = acc
            ml_ref[0, k] = jnp.where(lane == 0, m, l).T[0:8]
            return carry

        lax.fori_loop(0, kv_heads, head, 0)


def resp_kernel(meta_ref, q_ref, rk_hbm, acc_ref, ml_ref, out_ref, lse_ref, kv_buf, sems,
                *, rows, groups, kv_heads, scale, block, max_blocks):
    r = pl.program_id(0)
    c = meta_ref[meta_ref.shape[0] - 1]
    length = meta_ref[r]
    live_any = length > rows * c
    nrow = rows * groups
    kv_width = groups * HEAD
    limit = jnp.minimum(rows * c, length)
    nblocks = (limit + block - 1) // block

    @pl.when(jnp.logical_not(live_any))
    def _():
        out_ref[...] = jnp.zeros(out_ref.shape, out_ref.dtype)
        lse_ref[...] = jnp.zeros(lse_ref.shape, lse_ref.dtype)

    def run(n):
        width = n * block
        if n > 0:
            copies = [
                pltpu.make_async_copy(rk_hbm.at[h, r, pl.ds(0, width), :], kv_buf.at[h, pl.ds(0, width), :], sems.at[h])
                for h in range(2)
            ]
            for cp in copies:
                cp.start()
            for cp in copies:
                cp.wait()
        row_i = rows * c + lax.broadcasted_iota(jnp.int32, (nrow, 1), 0) % rows
        row_live = row_i < length

        def head(k, carry):
            col = pl.multiple_of(k * HEAD, HEAD)
            qoff = pl.multiple_of(k * kv_width, kv_width)
            t = ml_ref[0, k].T
            m = t[:, 0:1]
            l = t[:, 1:2]
            acc = acc_ref[0, k]
            if n > 0:
                qk = stack_groups(q_ref[0, :, pl.ds(qoff, kv_width)], groups)
                s = scores(qk, kv_buf[0, 0:width, pl.ds(col, HEAD)], scale)
                live = lax.broadcasted_iota(jnp.int32, (nrow, width), 1) < limit
                s = jnp.where(live, s, NEG)
                m_new = jnp.maximum(m, jnp.max(s, axis=-1, keepdims=True))
                alpha = jnp.exp(m - m_new)
                p = jnp.where(live, jnp.exp(s - m_new), 0.0)
                l = alpha * l + jnp.sum(p, axis=-1, keepdims=True)
                pv = jnp.dot(p.astype(jnp.bfloat16), kv_buf[1, 0:width, pl.ds(col, HEAD)],
                             preferred_element_type=jnp.float32)
                acc = alpha * acc + pv
                m = m_new
            o = jnp.where(row_live, acc / l, 0.0).astype(out_ref.dtype)
            for g in range(groups):
                out_ref[0, :, pl.ds(qoff + g * HEAD, HEAD)] = o[g * rows:(g + 1) * rows]
            lse = jnp.where(row_live, m + jnp.log(l), 0.0)
            lse_ref[0, k] = jnp.broadcast_to(lse, (nrow, 128)).T[0:1]
            return carry

        lax.fori_loop(0, kv_heads, head, 0)

    for n in range(max_blocks + 1):
        pl.when(live_any & (nblocks == n))(functools.partial(run, n))


def per_device(queries, prompt_kv, response_kv, lengths):
    resp_local, rows, width = queries.shape
    kv_width = prompt_kv.shape[2]
    kv_heads = kv_width // HEAD
    groups = width // kv_width
    nrow = rows * groups
    scale = 1.0 / math.sqrt(HEAD)
    c = lax.axis_index("ctx")
    meta = jnp.concatenate([lengths.astype(jnp.int32), c.astype(jnp.int32)[None]])

    full_prompt = lax.all_gather(lax.all_gather(prompt_kv, "ctx", axis=1, tiled=True), "resp", axis=1, tiled=True)
    full_resp = lax.all_gather(response_kv, "ctx", axis=2, tiled=True)
    n_prompt = full_prompt.shape[1]
    n_resp = full_resp.shape[2]

    q_spec = pl.BlockSpec((1, rows, width), lambda r, meta: (r, 0, 0))
    acc_spec = pl.BlockSpec((1, kv_heads, nrow, HEAD), lambda r, meta: (r, 0, 0, 0))
    ml_spec = pl.BlockSpec((1, kv_heads, 8, nrow), lambda r, meta: (r, 0, 0, 0))
    params = pltpu.CompilerParams(vmem_limit_bytes=48 * 1024 * 1024)
    acc, ml = pl.pallas_call(
        functools.partial(prompt_kernel, rows=rows, groups=groups, kv_heads=kv_heads, scale=scale),
        grid_spec=pltpu.PrefetchScalarGridSpec(
            num_scalar_prefetch=1,
            grid=(resp_local,),
            in_specs=[
                q_spec,
                pl.BlockSpec((2, n_prompt, kv_width), lambda r, meta: (0, 0, 0)),
                pl.BlockSpec((2, 1, rows, kv_width), lambda r, meta: (0, r, 0, 0)),
            ],
            out_specs=[acc_spec, ml_spec],
        ),
        out_shape=[
            jax.ShapeDtypeStruct((resp_local, kv_heads, nrow, HEAD), jnp.float32),
            jax.ShapeDtypeStruct((resp_local, kv_heads, 8, nrow), jnp.float32),
        ],
        compiler_params=params,
        cost_estimate=pl.CostEstimate(
            flops=4 * resp_local * kv_heads * nrow * (n_prompt + rows) * HEAD,
            transcendentals=resp_local * kv_heads * nrow * (n_prompt + rows),
            bytes_accessed=2 * (queries.size + full_prompt.size) + 4 * resp_local * kv_heads * nrow * HEAD,
        ),
    )(meta, queries, full_prompt, response_kv)

    block = 128
    max_blocks = (n_resp - rows + block - 1) // block
    attended, lse_t = pl.pallas_call(
        functools.partial(resp_kernel, rows=rows, groups=groups, kv_heads=kv_heads, scale=scale, block=block,
                          max_blocks=max_blocks),
        grid_spec=pltpu.PrefetchScalarGridSpec(
            num_scalar_prefetch=1,
            grid=(resp_local,),
            in_specs=[
                q_spec,
                pl.BlockSpec(memory_space=pl.ANY),
                acc_spec,
                ml_spec,
            ],
            out_specs=[
                q_spec,
                pl.BlockSpec((1, kv_heads, 1, nrow), lambda r, meta: (r, 0, 0, 0)),
            ],
            scratch_shapes=[
                pltpu.VMEM((2, max_blocks * block, kv_width), jnp.bfloat16),
                pltpu.SemaphoreType.DMA((2,)),
            ],
        ),
        out_shape=[
            jax.ShapeDtypeStruct(queries.shape, queries.dtype),
            jax.ShapeDtypeStruct((resp_local, kv_heads, 1, nrow), jnp.float32),
        ],
        compiler_params=params,
        cost_estimate=pl.CostEstimate(
            flops=4 * resp_local * kv_heads * nrow * n_resp * HEAD // 2,
            transcendentals=resp_local * kv_heads * nrow * n_resp // 2,
            bytes_accessed=2 * (2 * queries.size + full_resp.size) + 4 * resp_local * kv_heads * nrow * HEAD,
        ),
    )(meta, queries, full_resp, acc, ml)

    row_lse = (
        lse_t.reshape(resp_local, kv_heads, groups, rows)
        .transpose(0, 3, 1, 2)
        .reshape(resp_local, rows, kv_heads * groups)
    )
    return attended, row_lse


def solution(mesh):
    placed = (
        P("resp", "ctx", None),
        P(None, ("resp", "ctx"), None),
        P(None, "resp", "ctx", None),
        P("resp"),
    )
    return jax.shard_map(
        per_device,
        mesh=mesh,
        in_specs=placed,
        out_specs=(P("resp", "ctx", None), P("resp", "ctx", None)),
        check_vma=False,
    )
```

profile of v0, /device:TPU:1, one launch (start us, length us, event | category | flops | bytes accessed | tf_op | source)
XLA Modules:
  0.0 261.7 jit_solution(487134173684157490)
XLA Ops:
  7.2 0.0 all-gather.5.cloned.1.call-start
  7.2 30.5 %all_gather.10 = bf16[2,128,1024]{2,1,0:T(8,128)(2,1)} all-gather(bf16[2,8,1024]{2,1,0:T(8,128)(2,1)} %param.5), channel_id=1, replica_groups=mesh['resp'=8,'ctx'=16] {'ctx'}, dimensions={1}, use_global_device_ids=true | all-gather | bytes 557056 | tf_op jit(solution)/shard_map/all_gather | solution.py:128
  37.7 0.0 all-gather.5.cloned.1.call-update
  37.7 0.0 all-gather.3.cloned.1.call-start
  37.8 0.7 all-gather.3.cloned.1.call-update
  38.5 0.7 pad_add_fusion.meta_ref
  39.2 47.0 %all-gather.5.cloned.1.call-done.pk_ref = bf16[2,1024,1024]{2,1,0:T(8,128)(2,1)} async-done(((bf16[2,128,1024]{2,1,0:T(8,128)(2,1)}), bf16[2,1024,1024]{2,1,0:T(8,128)(2,1)}) %all-gather.5.cloned.1.call-update) | async-done | bytes 4194320 | tf_op jit(solution)/shard_map/all_gather | solution.py:128
  86.2 0.0 copy-start
  86.2 2.2 copy-done
  88.4 0.0 copy-start.2
  88.4 1.2 copy-done.2
  89.6 58.8 %shard_map.59 = (f32[8,8,256,128]{3,2,1,0:T(8,128)}, f32[8,8,8,256]{3,2,1,0:T(8,128)S(1)}) custom-call(s32[9]{0:T(128)S(1)} %pad_add_fusion.meta_ref, bf16[8,32,8192]{2,1,0:T(8,128)(2,1)S(1)} %copy-done, bf16[2,1024,1024]{2,1,0:T(8,128)(2,1)} %all-gather.5.cloned.1.call-done.pk_ref, bf16[2,8,32,1024]{3,2,1,0:T(8,128)(2,1)S(1)} %copy-done.2), custom_call_target="tpu_custom_call" | custom-call | flops 8858370048 | bytes 16777216 | tf_op jit(solution)/shard_map/pallas_call | solution.py:137
  148.5 48.4 %all-gather.3.cloned.1.call-done.rk_hbm = bf16[2,8,512,1024]{3,2,1,0:T(8,128)(2,1)} async-done(((bf16[2,8,32,1024]{3,2,1,0:T(8,128)(2,1)}), bf16[2,8,512,1024]{3,2,1,0:T(8,128)(2,1)}) %all-gather.3.cloned.1.call-update) | async-done | bytes 16777232 | tf_op jit(solution)/shard_map/all_gather | solution.py:129
  196.9 0.0 copy-start.1
  196.9 2.2 copy-done.1
  199.1 54.7 %shard_map.60 = (bf16[8,32,8192]{2,1,0:T(8,128)(2,1)}, f32[8,8,1,256]{3,2,1,0:T(1,128)S(1)}) custom-call(s32[9]{0:T(128)S(1)} %pad_add_fusion.meta_ref, bf16[8,32,8192]{2,1,0:T(8,128)(2,1)S(1)} %copy-done.1, bf16[2,8,512,1024]{3,2,1,0:T(8,128)(2,1)} %all-gather.3.cloned.1.call-done.rk_hbm, f32[8,8,256,128]{3,2,1,0:T(8,128)} %get-tuple-element.6.acc_ref, ...), custom_call_target="tpu_custom_call" | custom-call | flops 2147483648 | bytes 33554432 | tf_op jit(solution)/shard_map/pallas_call | solution.py:163
  253.8 0.2 reduce
  253.9 0.1 reshape.10
  254.1 0.8 copy.7
Async XLA Ops:
  7.2 79.0 %all-gather.5.cloned.1.call-start = ((), (), s32[]{:S(2)}) async-start(), calls=%async_computation.1 | async-start | bytes 4718592 | tf_op jit(solution)/shard_map/all_gather | solution.py:128
  37.7 159.2 %all-gather.3.cloned.1.call-start = ((), (), s32[]{:S(2)}) async-start(), calls=%async_computation | async-start | bytes 17825792 | tf_op jit(solution)/shard_map/all_gather | solution.py:129
  86.2 2.2 copy-start
  88.4 1.2 copy-start.2
  196.9 2.2 copy-start.1
Sparse Core Ops, SparseCore 0:
  37.9 48.3 all-gather.4
  88.7 108.2 all-gather.2
where the time goes:
time: 262 us
  Pallas kernels  114 us (44%)
  waiting for transfers between devices  96.2 us (37%)
  blocking collectives  30.5 us (12%)
  between operations  14.1 us (5%)
  local copies, waits for them, and re-layouts  6.49 us (2%)
    pallas_call x1, Pallas kernels, per_device(): pl.pallas_call(functools.partial(prompt_kernel, rows=rows, groups=groups,...  58.8 us
    pallas_call x1, Pallas kernels, per_device(): pl.pallas_call(functools.partial(resp_kernel, rows=rows, groups=groups, k...  54.7 us
    all_gather x1, waiting for transfers between devices, per_device(): full_resp = lax.all_gather(response_kv, 'ctx', axis=2, tiled=True)  48.4 us
    all_gather x1, waiting for transfers between devices, per_device(): lax.all_gather(lax.all_gather(prompt_kv, 'ctx', axis=1, tiled=True), 'res...  47 us
    all_gather x1, blocking collectives, per_device(): lax.all_gather(prompt_kv, 'ctx', axis=1, tiled=True)  30.5 us
    unnamed x7, local copies, waits for them, and re-layouts  6.39 us
  transfers between devices with their start and end apart: 2, of which 2 were waited for; matrix products, arithmetic and copies ran while one was open for 0% of the time, Pallas kernels for 22%

commit v1 on v0

--- a/solution.py
+++ b/solution.py
@@ -20,7 +20,7 @@
     return lax.dot_general(qk, keys, (((1,), (1,)), ((), ())), preferred_element_type=jnp.float32) * scale
 
 
-def prompt_kernel(meta_ref, q_ref, pk_ref, own_ref, acc_ref, ml_ref, *, rows, groups, kv_heads, scale):
+def prompt_kernel(meta_ref, q_ref, pk_ref, own_ref, acc_ref, m_ref, l_ref, *, rows, groups, kv_heads, scale):
     r = pl.program_id(0)
     c = meta_ref[meta_ref.shape[0] - 1]
     length = meta_ref[r]
@@ -32,7 +32,6 @@
         row_i = rows * c + lax.broadcasted_iota(jnp.int32, (nrow, 1), 0) % rows
         j = rows * c + lax.broadcasted_iota(jnp.int32, (nrow, rows), 1)
         live = (j <= row_i) & (j < length)
-        lane = lax.broadcasted_iota(jnp.int32, (nrow, 128), 1)
 
         def head(k, carry):
             col = pl.multiple_of(k * HEAD, HEAD)
@@ -46,13 +45,14 @@
             acc = jnp.dot(p1.astype(jnp.bfloat16), pk_ref[1, :, pl.ds(col, HEAD)], preferred_element_type=jnp.float32)
             acc = acc + jnp.dot(p2.astype(jnp.bfloat16), own_ref[1, 0, :, pl.ds(col, HEAD)], preferred_element_type=jnp.float32)
             acc_ref[0, k] = acc
-            ml_ref[0, k] = jnp.where(lane == 0, m, l).T[0:8]
+            m_ref[0, k] = jnp.broadcast_to(m, (nrow, HEAD))
+            l_ref[0, k] = jnp.broadcast_to(l, (nrow, HEAD))
             return carry
 
         lax.fori_loop(0, kv_heads, head, 0)
 
 
-def resp_kernel(meta_ref, q_ref, rk_hbm, acc_ref, ml_ref, out_ref, lse_ref, kv_buf, sems,
+def resp_kernel(meta_ref, q_ref, rk_hbm, acc_ref, m_ref, l_ref, out_ref, lse_ref, kv_buf, sems,
                 *, rows, groups, kv_heads, scale, block, max_blocks):
     r = pl.program_id(0)
     c = meta_ref[meta_ref.shape[0] - 1]
@@ -85,9 +85,8 @@
         def head(k, carry):
             col = pl.multiple_of(k * HEAD, HEAD)
             qoff = pl.multiple_of(k * kv_width, kv_width)
-            t = ml_ref[0, k].T
-            m = t[:, 0:1]
-            l = t[:, 1:2]
+            m = m_ref[0, k]
+            l = l_ref[0, k]
             acc = acc_ref[0, k]
             if n > 0:
                 qk = stack_groups(q_ref[0, :, pl.ds(qoff, kv_width)], groups)
@@ -96,7 +95,8 @@
                 s = jnp.where(live, s, NEG)
                 m_new = jnp.maximum(m, jnp.max(s, axis=-1, keepdims=True))
                 alpha = jnp.exp(m - m_new)
-                p = jnp.where(live, jnp.exp(s - m_new), 0.0)
+                m_wide = m_new if n == 1 else jnp.concatenate([m_new] * n, axis=1)
+                p = jnp.where(live, jnp.exp(s - m_wide), 0.0)
                 l = alpha * l + jnp.sum(p, axis=-1, keepdims=True)
                 pv = jnp.dot(p.astype(jnp.bfloat16), kv_buf[1, 0:width, pl.ds(col, HEAD)],
                              preferred_element_type=jnp.float32)
@@ -106,7 +106,7 @@
             for g in range(groups):
                 out_ref[0, :, pl.ds(qoff + g * HEAD, HEAD)] = o[g * rows:(g + 1) * rows]
             lse = jnp.where(row_live, m + jnp.log(l), 0.0)
-            lse_ref[0, k] = jnp.broadcast_to(lse, (nrow, 128)).T[0:1]
+            lse_ref[0, k] = lse.T[0:1]
             return carry
 
         lax.fori_loop(0, kv_heads, head, 0)
@@ -132,9 +132,9 @@
 
     q_spec = pl.BlockSpec((1, rows, width), lambda r, meta: (r, 0, 0))
     acc_spec = pl.BlockSpec((1, kv_heads, nrow, HEAD), lambda r, meta: (r, 0, 0, 0))
-    ml_spec = pl.BlockSpec((1, kv_heads, 8, nrow), lambda r, meta: (r, 0, 0, 0))
+
     params = pltpu.CompilerParams(vmem_limit_bytes=48 * 1024 * 1024)
-    acc, ml = pl.pallas_call(
+    acc, m_rep, l_rep = pl.pallas_call(
         functools.partial(prompt_kernel, rows=rows, groups=groups, kv_heads=kv_heads, scale=scale),
         grid_spec=pltpu.PrefetchScalarGridSpec(
             num_scalar_prefetch=1,
@@ -144,11 +144,12 @@
                 pl.BlockSpec((2, n_prompt, kv_width), lambda r, meta: (0, 0, 0)),
                 pl.BlockSpec((2, 1, rows, kv_width), lambda r, meta: (0, r, 0, 0)),
             ],
-            out_specs=[acc_spec, ml_spec],
+            out_specs=[acc_spec, acc_spec, acc_spec],
         ),
         out_shape=[
             jax.ShapeDtypeStruct((resp_local, kv_heads, nrow, HEAD), jnp.float32),
-            jax.ShapeDtypeStruct((resp_local, kv_heads, 8, nrow), jnp.float32),
+            jax.ShapeDtypeStruct((resp_local, kv_heads, nrow, HEAD), jnp.float32),
+            jax.ShapeDtypeStruct((resp_local, kv_heads, nrow, HEAD), jnp.float32),
         ],
         compiler_params=params,
         cost_estimate=pl.CostEstimate(
@@ -170,7 +171,8 @@
                 q_spec,
                 pl.BlockSpec(memory_space=pl.ANY),
                 acc_spec,
-                ml_spec,
+                acc_spec,
+                acc_spec,
             ],
             out_specs=[
                 q_spec,
@@ -191,7 +193,7 @@
             transcendentals=resp_local * kv_heads * nrow * n_resp // 2,
             bytes_accessed=2 * (2 * queries.size + full_resp.size) + 4 * resp_local * kv_heads * nrow * HEAD,
         ),
-    )(meta, queries, full_resp, acc, ml)
+    )(meta, queries, full_resp, acc, m_rep, l_rep)
 
     row_lse = (
         lse_t.reshape(resp_local, kv_heads, groups, rows)

time: 262 us -> 253 us (0.966)
  Pallas kernels: 114 us -> 107 us
    pallas_call x1, Pallas kernels: 54.7 us -> 46 us  [per_device(): pl.pallas_call(functools.partial(resp_kernel, rows=rows, groups=groups, k...]
  transfers between devices with their start and end apart: 2 -> 2, of which waited for: 2 -> 2; matrix products, arithmetic and copies ran while one was open for 0% -> 0% of each run, Pallas kernels for 22% -> 24%
where the time goes in v1:
time: 253 us
  Pallas kernels  107 us (42%)
  waiting for transfers between devices  94.4 us (37%)
  blocking collectives  30.5 us (12%)
  between operations  14.1 us (6%)
  local copies, waits for them, and re-layouts  6.49 us (3%)
    pallas_call x1, Pallas kernels, per_device(): pl.pallas_call(functools.partial(prompt_kernel, rows=rows, groups=groups,...  60.6 us
    all_gather x1, waiting for transfers between devices, per_device(): lax.all_gather(lax.all_gather(prompt_kv, 'ctx', axis=1, tiled=True), 'res...  47 us
    all_gather x1, waiting for transfers between devices, per_device(): full_resp = lax.all_gather(response_kv, 'ctx', axis=2, tiled=True)  46.7 us
    pallas_call x1, Pallas kernels, per_device(): pl.pallas_call(functools.partial(resp_kernel, rows=rows, groups=groups, k...  46 us
    all_gather x1, blocking collectives, per_device(): lax.all_gather(prompt_kv, 'ctx', axis=1, tiled=True)  30.5 us
    unnamed x7, local copies, waits for them, and re-layouts  6.39 us
  transfers between devices with their start and end apart: 2, of which 2 were waited for; matrix products, arithmetic and copies ran while one was open for 0% of the time, Pallas kernels for 24%

profile of v1, /device:TPU:1, one launch (start us, length us, event | category | flops | bytes accessed | tf_op | source)
XLA Modules:
  0.0 253.0 jit_solution(5292479491640659059)
XLA Ops:
  7.2 0.0 all-gather.5.cloned.1.call-start
  7.2 30.5 %all_gather.10 = bf16[2,128,1024]{2,1,0:T(8,128)(2,1)} all-gather(bf16[2,8,1024]{2,1,0:T(8,128)(2,1)} %param.5), channel_id=1, replica_groups=mesh['resp'=8,'ctx'=16] {'ctx'}, dimensions={1}, use_global_device_ids=true | all-gather | bytes 557056 | tf_op jit(solution)/shard_map/all_gather | solution.py:128
  37.7 0.0 all-gather.5.cloned.1.call-update
  37.7 0.0 all-gather.3.cloned.1.call-start
  37.8 0.7 all-gather.3.cloned.1.call-update
  38.5 0.7 pad_add_fusion.meta_ref
  39.2 47.0 %all-gather.5.cloned.1.call-done.pk_ref = bf16[2,1024,1024]{2,1,0:T(8,128)(2,1)} async-done(((bf16[2,128,1024]{2,1,0:T(8,128)(2,1)}), bf16[2,1024,1024]{2,1,0:T(8,128)(2,1)}) %all-gather.5.cloned.1.call-update) | async-done | bytes 4194320 | tf_op jit(solution)/shard_map/all_gather | solution.py:128
  86.2 0.0 copy-start
  86.2 2.2 copy-done
  88.4 0.0 copy-start.2
  88.4 1.2 copy-done.2
  89.6 60.6 %shard_map.59 = (f32[8,8,256,128]{3,2,1,0:T(8,128)}, f32[8,8,256,128]{3,2,1,0:T(8,128)}, f32[8,8,256,128]{3,2,1,0:T(8,128)}) custom-call(s32[9]{0:T(128)S(1)} %pad_add_fusion.meta_ref, bf16[8,32,8192]{2,1,0:T(8,128)(2,1)S(1)} %copy-done, bf16[2,1024,1024]{2,1,0:T(8,128)(2,1)} %all-gather.5.cloned.1.call-done.pk_ref, bf16[2,8,32,1024]{3,2,1,0:T(8,128)(2,1)S(1)} %copy-done.2), custom_call_target="tpu_custom_call" | custom-call | flops 8858370048 | bytes 16777216 | tf_op jit(solution)/shard_map/pallas_call | solution.py:137
  150.2 46.7 %all-gather.3.cloned.1.call-done.rk_hbm = bf16[2,8,512,1024]{3,2,1,0:T(8,128)(2,1)} async-done(((bf16[2,8,32,1024]{3,2,1,0:T(8,128)(2,1)}), bf16[2,8,512,1024]{3,2,1,0:T(8,128)(2,1)}) %all-gather.3.cloned.1.call-update) | async-done | bytes 16777232 | tf_op jit(solution)/shard_map/all_gather | solution.py:129
  196.9 0.0 copy-start.1
  196.9 2.2 copy-done.1
  199.1 46.0 %shard_map.60 = (bf16[8,32,8192]{2,1,0:T(8,128)(2,1)}, f32[8,8,1,256]{3,2,1,0:T(1,128)S(1)}) custom-call(s32[9]{0:T(128)S(1)} %pad_add_fusion.meta_ref, bf16[8,32,8192]{2,1,0:T(8,128)(2,1)S(1)} %copy-done.1, bf16[2,8,512,1024]{3,2,1,0:T(8,128)(2,1)} %all-gather.3.cloned.1.call-done.rk_hbm, f32[8,8,256,128]{3,2,1,0:T(8,128)} %get-tuple-element.7.acc_ref, ...), custom_call_target="tpu_custom_call" | custom-call | flops 2147483648 | bytes 33554432 | tf_op jit(solution)/shard_map/pallas_call | solution.py:164
  245.1 0.2 reduce
  245.3 0.1 reshape.10
  245.4 0.8 copy.7
Async XLA Ops:
  7.2 79.0 %all-gather.5.cloned.1.call-start = ((), (), s32[]{:S(2)}) async-start(), calls=%async_computation.1 | async-start | bytes 4718592 | tf_op jit(solution)/shard_map/all_gather | solution.py:128
  37.7 159.2 %all-gather.3.cloned.1.call-start = ((), (), s32[]{:S(2)}) async-start(), calls=%async_computation | async-start | bytes 17825792 | tf_op jit(solution)/shard_map/all_gather | solution.py:129
  86.2 2.2 copy-start
  88.4 1.2 copy-start.2
  196.9 2.2 copy-start.1
Sparse Core Ops, SparseCore 0:
  37.9 48.3 all-gather.4
  88.7 108.2 all-gather.2
